TPU v7x, 256 devices: a whole 4x4x8 slice. The times are simulated.
256 devices in a mesh: dp: 8 (over x, z_hi), tensor: 32 (over y, z_lo, core).
Axes of the slice: x: 4, y: 4, z: 8 (z_hi: 2, z_lo: 4; z = z_hi * 4 + z_lo), core: 2. Of those that a mesh axis runs over, the one named last changes fastest.
Arguments:
- tokens: bfloat16 [8, 4096, 1280], P('dp', 'tensor'), may hold values from -6 to 6
- segment_ids: int32 [8, 4096], P('dp', 'tensor'), may hold values from 0 to 3, never falling along the last dimension, each value on 1 to 2048 neighbouring positions
- pack_of_group: int32 [32], replicated, may hold values from 0 to 31, each once
- w_qkv: bfloat16 [1280, 1920], replicated, may hold values from -0.11320094 to 0.11320094
- qk_gain: float32 [640], replicated, may hold values from 0.5 to 7
- w_out: bfloat16 [640, 1280], replicated, may hold values from -0.25 to 0.25
- alpha_attn: float32 [1280], replicated, may hold values from 0.05 to 0.6
- w_up: bfloat16 [1280, 5120], P(None, 'dp'), may hold values from -0.15625 to 0.15625
- w_gate: bfloat16 [1280, 5120], P(None, 'dp'), may hold values from -0.15625 to 0.15625
- up_gain: float32 [5120], P('dp'), may hold values from 0.5 to 2
- gate_gain: float32 [5120], P('dp'), may hold values from 0.5 to 2
- w_down: bfloat16 [5120, 1280], P('dp'), may hold values from -0.078125 to 0.078125
- alpha_mlp: float32 [1280], replicated, may hold values from 0.05 to 0.6
- w_vocab: bfloat16 [1280, 32000], P(None, ('dp', 'tensor')), may hold values from -0.15625 to 0.15625
- logit_gain: bfloat16 [32000], P(('dp', 'tensor')), may hold values from 1 to 10
Outputs:
- result_rows: bfloat16 [8, 4096, 1280], P('dp', 'tensor')
- request_norm: float32 [32], replicated
- max_logit: float32 [32], replicated
Inputs may be any that keep to these rules, and one draw needn't show every extreme that they name: `segment_ids`: within a pack the request numbers never fall, every request 0 to 3 has one or more tokens, and one request has exactly 2048 tokens.
All inputs are finite; a program needn't handle non-finite values.
Results may differ from a plain program's by a relative error of at most 0.013.
Values may be sent and summed in bfloat16 or wider, within the bound.
No kernel may reach another device: no remote copies, remote signals or barrier semaphores. Data moves between devices by JAX's collectives and lax.ppermute only.
A program may use at most 128 MiB of HBM per device.

v0:
```python
import math
import jax
import jax.numpy as jnp
from jax import lax
from jax.sharding import PartitionSpec as P

HEADS = 10
HD = 64
REQS = 4
EPSILON = 1e-06
NEGATIVE = -1e30


def normalize(values):
    return values * lax.rsqrt(jnp.mean(values * values, axis=-1, keepdims=True) + EPSILON)


def head_norm(values, qk_gain):
    reshaped = values.reshape(values.shape[0], HEADS, HD)
    return (normalize(reshaped) * qk_gain.reshape(HEADS, HD)).astype(jnp.bfloat16)


def local(
    tokens,
    segment_ids,
    pack_of_group,
    w_qkv,
    qk_gain,
    w_out,
    alpha_attn,
    w_up,
    w_gate,
    up_gain,
    gate_gain,
    w_down,
    alpha_mlp,
    w_vocab,
    logit_gain,
):
    row_count = tokens.shape[1]
    head_width = HEADS * HD
    segments = segment_ids[0]
    tensor_index = lax.axis_index("tensor")
    positions = tensor_index * row_count + jnp.arange(row_count, dtype=jnp.int32)
    request_numbers = jnp.arange(REQS, dtype=jnp.int32)
    start_rows = normalize(tokens[0].astype(jnp.float32)).astype(jnp.bfloat16)
    projected = jnp.dot(start_rows, w_qkv, preferred_element_type=jnp.float32)
    queries = head_norm(projected[:, :head_width], qk_gain)
    key_rows = head_norm(projected[:, head_width : 2 * head_width], qk_gain).reshape(
        row_count, head_width
    )
    value_rows = projected[:, 2 * head_width :].astype(jnp.bfloat16)
    score_scale = 1.0 / math.sqrt(HD)
    packed = jnp.concatenate([key_rows, value_rows], axis=1)
    gathered = lax.all_gather(packed, "tensor", axis=0, tiled=False)
    vocab_pack = jnp.concatenate(
        [w_vocab, logit_gain[None], jnp.zeros((7, w_vocab.shape[1]), w_vocab.dtype)], axis=0
    )
    vocab_pack, gathered = lax.optimization_barrier((vocab_pack, gathered))
    vocab_all = lax.all_gather(vocab_pack, "dp", axis=0, tiled=False)
    key_all = gathered[:, :row_count, :head_width].reshape(-1, head_width)
    value_all = gathered[:, :row_count, head_width:].reshape(-1, head_width)
    seg_all = lax.all_gather(segments, "tensor", axis=0, tiled=True)
    tally = jnp.sum((seg_all[:, None] == request_numbers[None, :]).astype(jnp.int32), axis=0)
    total_keys = key_all.shape[0]
    key_pos = jnp.arange(total_keys, dtype=jnp.int32)
    head_of_column = jnp.arange(head_width, dtype=jnp.int32) // HD
    head_mask = (jnp.arange(HEADS, dtype=jnp.int32)[:, None] == head_of_column[None, :]).astype(
        jnp.bfloat16
    )
    query_flat = queries.reshape(row_count, head_width)
    query_blocks = (query_flat[None, :, :] * head_mask[:, None, :]).reshape(
        HEADS * row_count, head_width
    )
    scores = (
        lax.dot_general(
            query_blocks, key_all, (((1,), (1,)), ((), ())), preferred_element_type=jnp.float32
        ).reshape(HEADS, row_count, total_keys)
        * score_scale
    )
    allowed = (seg_all[None, :] == segments[:, None]) & (key_pos[None, :] <= positions[:, None])
    row_max = jnp.max(jnp.where(allowed[None], scores, NEGATIVE), axis=2)
    weights = jnp.where(allowed[None], jnp.exp(scores - row_max[:, :, None]), 0.0)
    weight_sum = jnp.sum(weights, axis=2)
    weighted = jnp.dot(
        weights.astype(jnp.bfloat16).reshape(HEADS * row_count, total_keys),
        value_all,
        preferred_element_type=jnp.float32,
    ).reshape(HEADS, row_count, head_width)
    attended = jnp.sum(
        weighted / weight_sum[:, :, None] * head_mask[:, None, :].astype(jnp.float32), axis=0
    ).astype(jnp.bfloat16)
    attn_rows = normalize(jnp.dot(attended, w_out, preferred_element_type=jnp.float32))
    residual_in = start_rows.astype(jnp.float32)
    mid_rows = normalize(residual_in + alpha_attn * (attn_rows - residual_in)).astype(jnp.bfloat16)
    mid_rows, vocab_all = lax.optimization_barrier((mid_rows, vocab_all))
    received = lax.all_gather(mid_rows, "dp", axis=0, tiled=True)
    up_proj = jnp.dot(received, w_up, preferred_element_type=jnp.float32) * up_gain
    gate_proj = jnp.dot(received, w_gate, preferred_element_type=jnp.float32) * gate_gain
    hidden = (up_proj * jax.nn.silu(gate_proj)).astype(jnp.bfloat16)
    mixed_sum = lax.psum_scatter(
        jnp.dot(hidden, w_down, preferred_element_type=jnp.float32).astype(jnp.bfloat16),
        "dp",
        scatter_dimension=0,
        tiled=True,
    ).astype(jnp.float32)
    mlp_rows = normalize(mixed_sum)
    residual_mid = mid_rows.astype(jnp.float32)
    result_rows = normalize(residual_mid + alpha_mlp * (mlp_rows - residual_mid)).astype(
        jnp.bfloat16
    )
    request_ends = jnp.cumsum(tally) - 1
    same_request = segments[:, None] == request_numbers[None, :]
    row_end = jnp.sum(jnp.where(same_request, request_ends[None, :], 0), axis=1)
    is_last = positions == row_end
    member = same_request.astype(jnp.float32)
    chosen = member * is_last[:, None].astype(jnp.float32)
    result_f32 = result_rows.astype(jnp.float32)
    row_sums = jnp.dot(
        member.T.astype(jnp.bfloat16), result_rows, preferred_element_type=jnp.float32
    )
    last_rows = jnp.dot(
        chosen.T.astype(jnp.bfloat16), result_rows, preferred_element_type=jnp.float32
    )
    partial = jnp.concatenate([row_sums, last_rows], axis=0)
    summed = jnp.sum(
        lax.all_gather(partial.astype(jnp.bfloat16), "tensor", axis=0, tiled=False).astype(
            jnp.float32
        ),
        axis=0,
    )
    row_sums, last_rows = (summed[:REQS], summed[REQS:])
    counts = tally.astype(jnp.float32)
    request_mean = row_sums / counts[:, None]
    group_norm = jnp.sqrt(jnp.mean(request_mean * request_mean, axis=1))
    slot_count = lax.axis_size("dp") * REQS
    dp_index = lax.axis_index("dp")
    model_width = last_rows.shape[1]
    pack_logits = jnp.einsum(
        "rd,gdc->rgc",
        last_rows.astype(jnp.bfloat16),
        vocab_all[:, :model_width],
        preferred_element_type=jnp.float32,
    ) * vocab_all[None, :, model_width].astype(jnp.float32)
    pack_max = jnp.max(pack_logits.reshape(REQS, -1), axis=1)
    own_slot = jnp.arange(slot_count, dtype=jnp.int32) // REQS == dp_index
    spread_max = jnp.where(own_slot, jnp.tile(pack_max, slot_count // REQS), NEGATIVE)
    spread_norm = jnp.where(own_slot, jnp.tile(group_norm, slot_count // REQS), NEGATIVE)
    every = lax.pmax(jnp.concatenate([spread_max, spread_norm]), ("dp", "tensor"))
    every_max, every_norm = (every[:slot_count], every[slot_count:])
    placement = (pack_of_group[:, None] == jnp.arange(slot_count, dtype=jnp.int32)[None, :]).astype(
        jnp.float32
    )
    request_norm = jnp.dot(every_norm, placement, precision=lax.Precision.HIGHEST)
    max_logit = jnp.dot(every_max, placement, precision=lax.Precision.HIGHEST)
    return (result_rows[None], request_norm, max_logit)


def solution(mesh):
    return jax.shard_map(
        local,
        mesh=mesh,
        in_specs=(
            P("dp", "tensor", None),
            P("dp", "tensor"),
            P(),
            P(),
            P(),
            P(),
            P(),
            P(None, "dp"),
            P(None, "dp"),
            P("dp"),
            P("dp"),
            P("dp", None),
            P(),
            P(None, ("dp", "tensor")),
            P(("dp", "tensor")),
        ),
        out_specs=(P("dp", "tensor", None), P(), P()),
        check_vma=False,
    )
```

profile of v0, /device:TPU:1, one launch (start us, length us, event | category | flops | bytes accessed | tf_op | source)
XLA Modules:
  0.0 512.1 jit_solution(1264424142614423006)
XLA Ops:
  7.2 0.0 copy-start
  7.2 0.0 all-gather.9.cloned.1.call-start
  7.2 1.2 fusion.30
  8.5 3.4 fusion.62
  11.9 0.0 copy-start.9
  12.0 0.9 copy.26
  12.9 1.0 reduce_sum.118
  13.9 0.0 copy-start.10
  13.9 0.9 copy.27
  14.8 0.2 copy.28
  15.1 0.2 copy.29
  15.3 0.0 copy-done.9
  15.3 1.0 multiply_convert_fusion.4
  16.3 0.8 pad_maximum_fusion
  17.1 0.0 all-gather.9.cloned.1.call-update
  17.1 0.0 all-gather.11.cloned.1.call-start
  17.2 3.1 concatenate.24
  20.3 46.1 %all-gather = s32[1,4096]{1,0:T(1,128)S(1)} all-gather(s32[1,128]{1,0:T(1,128)S(1)} %copy-done.8), channel_id=2, replica_groups=mesh['dp'=8,'tensor'=32] {'tensor'}, dimensions={1}, use_global_device_ids=true | all-gather | bytes 16896 | tf_op jit(solution)/shard_map/all_gather | solution.py:63
  66.4 0.5 fusion.14
  66.9 26.5 %all-gather.9.cloned.1.call-done = bf16[4096,1280]{1,0:T(8,128)(2,1)} async-done(((bf16[128,1280]{1,0:T(8,128)(2,1)}), bf16[4096,1280]{1,0:T(8,128)(2,1)}) %all-gather.9.cloned.1.call-update) | async-done | bytes 10485776 | tf_op jit(solution)/shard_map/all_gather | solution.py:55
  93.5 9.6 %fusion.64 = (bf16[32,128,640]{2,1,0:T(8,128)(2,1)}, bf16[32,128,640]{2,1,0:T(8,128)(2,1)}) fusion(bf16[32,128,1280]{2,1,0:T(8,128)(2,1)} %bitcast.58), kind=kLoop, calls=%fused_computation.115 | loop fusion | bytes 20971520 | tf_op jit(solution)/shard_map/slice | solution.py:61
  103.1 0.0 all-gather.11.cloned.1.call-update
  103.1 0.2 all-gather.7.cloned.1.call-start
  103.3 13.9 %fusion.17 = f32[10,128,4096]{2,1,0:T(8,128)} fusion(bf16[4096,640,1]{1,0,2:T(8,128)(2,1)} %bitcast.60, bf16[10,640]{1,0:T(8,128)(2,1)S(1)} %get-tuple-element.17, bf16[128,640]{1,0:T(8,128)(2,1)S(1)} %get-tuple-element.13), kind=kOutput, calls=%fused_computation.21 | convolution fusion | flops 6711705600 | bytes 26391040 | tf_op jit(solution)/shard_map/dot_general | solution.py:76
  117.3 21.3 %fusion.65 = f32[10,128]{1,0:T(8,128)S(1)} fusion(f32[10,128,4096]{2,1,0:T(8,128)} %fusion.17, pred[128,4096]{1,0:T(8,128)(4,1)S(1)} %fusion.14), kind=kOutput, calls=%fused_computation.116 | output fusion | flops 31461376 | bytes 21500928 | tf_op jit(solution)/shard_map/sub | solution.py:83
  138.6 0.0 copy-start.4
  138.6 0.0 copy-start.6
  138.6 25.4 %multiply_reduce_fusion = bf16[128,640]{1,0:T(8,128)(2,1)S(1)} fusion(bf16[4096,640,1]{1,0,2:T(8,128)(2,1)} %bitcast.59, f32[10,640]{1,0:T(8,128)S(1)} %get-tuple-element.18, f32[10,128]{1,0:T(8,128)S(1)} %fusion.65, f32[10,128,4096]{2,1,0:T(8,128)} %fusion.17, pred[128,4096]{1,0:T(8,128)(4,1)} %copy-done.5), kind=kOutput, calls=%fused_computation.11 | convolution fusion | flops 6744724480 | bytes 26933248 | tf_op jit(solution)/shard_map/dot_general | solution.py:85
  164.0 0.0 copy-start.1
  164.0 0.5 multiply_reduce_fusion.3
  164.6 0.4 copy-done.1
  165.0 0.3 multiply_reduce_fusion.2
  165.3 1.0 multiply_convert_fusion.2
  166.3 18.2 %all-gather.11.cloned.1.call-done = bf16[10304,125]{1,0:T(8,128)(2,1)} async-done(((bf16[1288,125]{1,0:T(8,128)(2,1)}), bf16[10304,125]{1,0:T(8,128)(2,1)}) %all-gather.11.cloned.1.call-update) | async-done | bytes 2576016 | tf_op jit(solution)/shard_map/all_gather | solution.py:60
  184.5 0.0 all-gather.7.cloned.1.call-update
  184.5 0.0 copy-start.12
  184.5 0.0 copy-start.13
  184.5 0.0 reduce-scatter.2.cloned.1.call-start
  184.6 82.3 %all-gather.7.cloned.1.call-done = bf16[1024,1280]{1,0:T(8,128)(2,1)} async-done(((bf16[128,1280]{1,0:T(8,128)(2,1)}), bf16[1024,1280]{1,0:T(8,128)(2,1)}) %all-gather.7.cloned.1.call-update) | async-done | bytes 2621456 | tf_op jit(solution)/shard_map/all_gather | solution.py:97
  266.9 5.4 %fusion.66 = f32[1024,640]{1,0:T(8,128)} fusion(bf16[1024,1280]{1,0:T(8,128)(2,1)} %all-gather.7.cloned.1.call-done, bf16[1280,640]{1,0:T(8,128)(2,1)S(1)} %copy-done.11), kind=kOutput, calls=%fused_computation.117 | convolution fusion | flops 1677721600 | bytes 6881280 | tf_op jit(solution)/shard_map/dot_general | solution.py:98
  272.3 8.9 %convolution_convert_fusion = bf16[1024,1280]{1,0:T(8,128)(2,1)} fusion(bf16[640,1280]{1,0:T(8,128)(2,1)S(1)} %copy-done, f32[1024,640]{1,0:T(8,128)} %fusion.66, bf16[1024,1280]{1,0:T(8,128)(2,1)} %all-gather.7.cloned.1.call-done, bf16[1280,640]{1,0:T(8,128)(2,1)} %param.23, f32[640]{0:T(1024)S(1)} %copy-done.12, f32[640]{0:T(1024)S(1)} %copy-done.13), kind=kOutput, calls=%fused_computation.10 | convolution fusion | flops 3361996800 | bytes 11146240 | tf_op jit(solution)/shard_map/dot_general | solution.py:102
  281.3 0.0 reduce-scatter.2.cloned.1.call-update
  281.3 0.1 convert_reduce_fusion.1
  281.4 0.2 reduce-window.8
  281.6 0.1 select_reduce_fusion.1
  281.7 0.7 slice_convert_fusion.2
  282.4 95.8 %reduce-scatter.2.cloned.1.call-done = bf16[128,1280]{1,0:T(8,128)(2,1)} async-done(((bf16[1024,1280]{1,0:T(8,128)(2,1)}), bf16[128,1280]{1,0:T(8,128)(2,1)}) %reduce-scatter.2.cloned.1.call-update) | async-done | bytes 327696 | tf_op jit(solution)/shard_map/reduce_scatter | solution.py:101
  378.3 1.1 fusion.29
  379.4 1.3 multiply_reduce_fusion.1
  380.8 1.4 multiply_convert_fusion.1
  382.1 0.0 copy-start.3
  382.1 0.0 copy-start.14
  382.1 0.2 fusion.12
  382.3 0.2 fusion.13
  382.5 45.7 %all_gather.28 = bf16[32,8,1280]{2,1,0:T(8,128)(2,1)S(1)} all-gather(bf16[1,8,1280]{2,1,0:T(8,128)(2,1)S(1)} %pad_maximum_fusion.1), channel_id=1, replica_groups=mesh['dp'=8,'tensor'=32] {'tensor'}, dimensions={0}, use_global_device_ids=true | all-gather | bytes 675840 | tf_op jit(solution)/shard_map/all_gather | solution.py:127
  428.2 0.1 convert_reduce_fusion
  428.3 0.2 fusion.39
  428.5 0.1 tile.21
  428.6 2.3 fusion.22
  430.9 0.1 tile.9
  431.0 0.1 pad_maximum_fusion.2
  431.1 73.0 %pmax.7 = f32[64]{0:T(128)S(1)} all-reduce(f32[64]{0:T(128)S(1)} %pad_maximum_fusion.2), channel_id=1, replica_groups=mesh['dp'=8,'tensor'=32] {'dp','tensor'}, use_global_device_ids=true, to_apply=%region_17.18 | all-reduce | flops 64 | bytes 512 | tf_op jit(solution)/shard_map/pmax | solution.py:149
  504.1 0.7 convolution_bitcast_fusion.1
  504.8 0.7 convolution_bitcast_fusion
  (42 shorter events, 0.3 us)
Async XLA Ops:
  7.2 265.2 %copy-start = (bf16[640,1280]{1,0:T(8,128)(2,1)S(1)}, bf16[640,1280]{1,0:T(8,128)(2,1)}, u32[]{:S(2)}) copy-start(bf16[640,1280]{1,0:T(8,128)(2,1)} %param.26) | copy-start | bytes 4915204
  7.2 86.3 %all-gather.9.cloned.1.call-start = ((), (), s32[]{:S(2)}) async-start(), calls=%async_computation.3 | async-start | bytes 10813440 | tf_op jit(solution)/shard_map/all_gather | solution.py:55
  11.9 3.3 copy-start.9
  13.9 3.2 copy-start.10
  14.8 5.4 %copy-start.8 = (s32[1,128]{1,0:T(1,128)S(1)}, s32[1,128]{1,0:T(1,128)}, u32[]{:S(2)}) copy-start(s32[1,128]{1,0:T(1,128)} %param.16) | copy-start | bytes 1540
  17.1 167.4 %all-gather.11.cloned.1.call-start = ((), (), s32[]{:S(2)}) async-start(), calls=%async_computation.4 | async-start | bytes 2967552 | tf_op jit(solution)/shard_map/all_gather | solution.py:60
  66.9 50.4 %copy-start.5 = (pred[128,4096]{1,0:T(8,128)(4,1)}, pred[128,4096]{1,0:T(8,128)(4,1)S(1)}, u32[]{:S(2)}) copy-start(pred[128,4096]{1,0:T(8,128)(4,1)S(1)} %fusion.14) | copy-start | bytes 1572868
  103.1 163.8 %all-gather.7.cloned.1.call-start = ((), (), s32[]{:S(2)}) async-start(), calls=%async_computation.1 | async-start | bytes 2949120 | tf_op jit(solution)/shard_map/all_gather | solution.py:97
  138.6 25.4 %copy-start.4 = (bf16[640,1280]{1,0:T(8,128)(2,1)S(1)}, bf16[640,1280]{1,0:T(8,128)(2,1)}, u32[]{:S(2)}) copy-start(bf16[640,1280]{1,0:T(8,128)(2,1)} %param.20) | copy-start | bytes 4915204
  138.6 25.9 %copy-start.6 = (f32[1280]{0:T(1024)S(1)}, f32[1280]{0:T(1024)}, u32[]{:S(2)}) copy-start(f32[1280]{0:T(1024)} %param.21) | copy-start | bytes 15364
  164.0 1.0 copy-start.1
  164.5 102.4 %copy-start.11 = (bf16[1280,640]{1,0:T(8,128)(2,1)S(1)}, bf16[1280,640]{1,0:T(8,128)(2,1)}, u32[]{:S(2)}) copy-start(bf16[1280,640]{1,0:T(8,128)(2,1)} %param.22) | copy-start | bytes 4915204
  184.5 87.8 %copy-start.12 = (f32[640]{0:T(1024)S(1)}, f32[640]{0:T(1024)}, u32[]{:S(2)}) copy-start(f32[640]{0:T(1024)} %param.25) | copy-start | bytes 7684
  184.5 87.8 %copy-start.13 = (f32[640]{0:T(1024)S(1)}, f32[640]{0:T(1024)}, u32[]{:S(2)}) copy-start(f32[640]{0:T(1024)} %param.24) | copy-start | bytes 7684
  184.5 193.7 %reduce-scatter.2.cloned.1.call-start = ((), (), s32[]{:S(2)}) async-start(), calls=%async_computation.2 | async-start | bytes 2949120 | tf_op jit(solution)/shard_map/reduce_scatter | solution.py:101
  281.3 98.2 %copy-start.2 = (bf16[128,1280]{1,0:T(8,128)(2,1)S(1)}, bf16[128,1280]{1,0:T(8,128)(2,1)}, u32[]{:S(2)}) copy-start(bf16[128,1280]{1,0:T(8,128)(2,1)} %multiply_convert_fusion.2) | copy-start | bytes 983044
  281.3 98.2 %copy-start.7 = (f32[1280]{0:T(1024)S(1)}, f32[1280]{0:T(1024)}, u32[]{:S(2)}) copy-start(f32[1280]{0:T(1024)} %param.27) | copy-start | bytes 15364
  382.1 123.4 %copy-start.3 = (bf16[128,1280]{1,0:T(8,128)(2,1)}, bf16[128,1280]{1,0:T(8,128)(2,1)S(1)}, u32[]{:S(2)}) copy-start(bf16[128,1280]{1,0:T(8,128)(2,1)S(1)} %multiply_convert_fusion.1) | copy-start | bytes 983044
  382.1 122.0 %copy-start.14 = (s32[32]{0:T(128)S(1)}, s32[32]{0:T(128)}, u32[]{:S(2)}) copy-start(s32[32]{0:T(128)} %param.17) | copy-start | bytes 388
Sparse Core Ops, SparseCore 0:
  17.2 76.2 all-gather.8
  103.2 81.2 all-gather.10
  187.7 79.1 all-gather.6
  281.4 96.8 reduce-scatter.1
where the time goes:
time: 513 us; the launch traced here: 512 us
  waiting for transfers between devices  223 us (43%)
  blocking collectives  165 us (32%)
  matrix products  61.7 us (12%)
  other arithmetic  32.6 us (6%)
  local copies, waits for them, and re-layouts  15.6 us (3%)
  between operations  14.1 us (3%)
    reduce_scatter x1, waiting for transfers between devices, local(): lax.psum_scatter(jnp.dot(hidden, w_down, preferred_element_type=jnp.float...  95.8 us
    all_gather x1, waiting for transfers between devices, local(): received = lax.all_gather(mid_rows, 'dp', axis=0, tiled=True)  82.3 us
    pmax x1, blocking collectives, local(): lax.pmax(jnp.concatenate([spread_max, spread_norm]), ('dp', 'tensor'))  73 us
    all_gather x1, blocking collectives, local(): seg_all = lax.all_gather(segments, 'tensor', axis=0, tiled=True)  46.1 us
    all_gather x1, blocking collectives, local(): lax.all_gather(partial.astype(jnp.bfloat16), 'tensor', axis=0, tiled=False)  45.7 us
    all_gather x1, waiting for transfers between devices, local(): gathered = lax.all_gather(packed, 'tensor', axis=0, tiled=False)  26.5 us
    dot_general x1, matrix products, local(): jnp.dot(weights.astype(jnp.bfloat16).reshape(HEADS * row_count, total_key...  25.4 us
    sub x1, other arithmetic, local(): scores - row_max[:, :, None]  21.3 us
  transfers between devices with their start and end apart: 4, of which 4 were waited for; matrix products, arithmetic and copies ran while one was open for 13% of the time, Pallas kernels for 0%

commit v1 on v0

--- a/solution.py
+++ b/solution.py
@@ -94,7 +94,9 @@
     residual_in = start_rows.astype(jnp.float32)
     mid_rows = normalize(residual_in + alpha_attn * (attn_rows - residual_in)).astype(jnp.bfloat16)
     mid_rows, vocab_all = lax.optimization_barrier((mid_rows, vocab_all))
-    received = lax.all_gather(mid_rows, "dp", axis=0, tiled=True)
+    received = jnp.concatenate(
+        lax.all_to_all(jnp.stack([mid_rows] * lax.axis_size("dp")), "dp", 0, 0), axis=0
+    )
     up_proj = jnp.dot(received, w_up, preferred_element_type=jnp.float32) * up_gain
     gate_proj = jnp.dot(received, w_gate, preferred_element_type=jnp.float32) * gate_gain
     hidden = (up_proj * jax.nn.silu(gate_proj)).astype(jnp.bfloat16)

time: 513 us -> 497 us (0.969)
  waiting for transfers between devices: 223 us -> 172 us
  blocking collectives: 165 us -> 201 us
    all_gather x1 -> x0, waiting for transfers between devices: 82.3 us -> none  [local(): received = lax.all_gather(mid_rows, 'dp', axis=0, tiled=True)]
    all_to_all x0 -> x1, blocking collectives: none -> 36.4 us  [local(): lax.all_to_all(jnp.stack([mid_rows] * lax.axis_size('dp')), 'dp', 0, 0)]
    reduce_scatter x1, waiting for transfers between devices: 95.8 us -> 126 us  [local(): lax.psum_scatter(jnp.dot(hidden, w_down, preferred_element_type=jnp.float...]
  transfers between devices with their start and end apart: 4 -> 3, of which waited for: 4 -> 3; matrix products, arithmetic and copies ran while one was open for 13% -> 13% of each run, Pallas kernels for 0% -> 0%
where the time goes in v1:
time: 497 us; the launch traced here: 496 us
  blocking collectives  201 us (40%)
  waiting for transfers between devices  172 us (35%)
  matrix products  60 us (12%)
  other arithmetic  31.9 us (6%)
  local copies, waits for them, and re-layouts  17.3 us (3%)
  between operations  14 us (3%)
    reduce_scatter x1, waiting for transfers between devices, local(): lax.psum_scatter(jnp.dot(hidden, w_down, preferred_element_type=jnp.float...  126 us
    pmax x1, blocking collectives, local(): lax.pmax(jnp.concatenate([spread_max, spread_norm]), ('dp', 'tensor'))  73 us
    all_gather x1, blocking collectives, local(): seg_all = lax.all_gather(segments, 'tensor', axis=0, tiled=True)  46.1 us
    all_gather x1, blocking collectives, local(): lax.all_gather(partial.astype(jnp.bfloat16), 'tensor', axis=0, tiled=False)  45.6 us
    all_to_all x1, blocking collectives, local(): lax.all_to_all(jnp.stack([mid_rows] * lax.axis_size('dp')), 'dp', 0, 0)  36.4 us
    all_gather x1, waiting for transfers between devices, local(): gathered = lax.all_gather(packed, 'tensor', axis=0, tiled=False)  26.5 us
    dot_general x1, matrix products, local(): jnp.dot(weights.astype(jnp.bfloat16).reshape(HEADS * row_count, total_key...  25.4 us
    sub x1, other arithmetic, local(): scores - row_max[:, :, None]  21.3 us
  transfers between devices with their start and end apart: 3, of which 3 were waited for; matrix products, arithmetic and copies ran while one was open for 13% of the time, Pallas kernels for 0%

profile of v1, /device:TPU:1, one launch (start us, length us, event | category | flops | bytes accessed | tf_op | source)
XLA Modules:
  0.0 496.5 jit_solution(5060930470565189501)
XLA Ops:
  7.2 0.0 copy-start
  7.2 0.0 all-gather.6.cloned.1.call-start
  7.2 1.2 fusion.30
  8.5 3.4 fusion.62
  11.9 0.0 copy-start.9
  12.0 0.9 copy.26
  12.9 1.0 reduce_sum.118
  13.9 0.0 copy-start.10
  13.9 0.9 copy.27
  14.8 0.2 copy.28
  15.1 0.2 copy.29
  15.3 0.0 copy-done.9
  15.3 1.0 multiply_convert_fusion.4
  16.3 0.8 pad_maximum_fusion
  17.1 0.0 all-gather.6.cloned.1.call-update
  17.1 0.0 all-gather.8.cloned.1.call-start
  17.2 3.1 concatenate.24
  20.3 46.1 %all-gather = s32[1,4096]{1,0:T(1,128)S(1)} all-gather(s32[1,128]{1,0:T(1,128)S(1)} %copy-done.8), channel_id=2, replica_groups=mesh['dp'=8,'tensor'=32] {'tensor'}, dimensions={1}, use_global_device_ids=true | all-gather | bytes 16896 | tf_op jit(solution)/shard_map/all_gather | solution.py:63
  66.4 0.5 fusion.14
  66.9 0.0 copy-start.5
  66.9 26.5 %all-gather.6.cloned.1.call-done = bf16[4096,1280]{1,0:T(8,128)(2,1)} async-done(((bf16[128,1280]{1,0:T(8,128)(2,1)}), bf16[4096,1280]{1,0:T(8,128)(2,1)}) %all-gather.6.cloned.1.call-update) | async-done | bytes 10485776 | tf_op jit(solution)/shard_map/all_gather | solution.py:55
  93.5 9.6 %fusion.64 = (bf16[32,128,640]{2,1,0:T(8,128)(2,1)}, bf16[32,128,640]{2,1,0:T(8,128)(2,1)}) fusion(bf16[32,128,1280]{2,1,0:T(8,128)(2,1)} %bitcast.59), kind=kLoop, calls=%fused_computation.115 | loop fusion | bytes 20971520 | tf_op jit(solution)/shard_map/slice | solution.py:61
  103.1 0.0 all-gather.8.cloned.1.call-update
  103.1 0.2 reduce-scatter.2.cloned.1.call-start
  103.3 13.9 %fusion.17 = f32[10,128,4096]{2,1,0:T(8,128)} fusion(bf16[4096,640,1]{1,0,2:T(8,128)(2,1)} %bitcast.61, bf16[10,640]{1,0:T(8,128)(2,1)S(1)} %get-tuple-element.17, bf16[128,640]{1,0:T(8,128)(2,1)S(1)} %get-tuple-element.13), kind=kOutput, calls=%fused_computation.21 | convolution fusion | flops 6711705600 | bytes 26391040 | tf_op jit(solution)/shard_map/dot_general | solution.py:76
  117.3 21.3 %fusion.65 = f32[10,128]{1,0:T(8,128)S(1)} fusion(f32[10,128,4096]{2,1,0:T(8,128)} %fusion.17, pred[128,4096]{1,0:T(8,128)(4,1)S(1)} %fusion.14), kind=kOutput, calls=%fused_computation.116 | output fusion | flops 31461376 | bytes 21500928 | tf_op jit(solution)/shard_map/sub | solution.py:83
  138.6 0.0 copy-start.4
  138.6 0.0 copy-start.6
  138.6 25.4 %multiply_reduce_fusion = bf16[128,640]{1,0:T(8,128)(2,1)S(1)} fusion(bf16[4096,640,1]{1,0,2:T(8,128)(2,1)} %bitcast.60, f32[10,640]{1,0:T(8,128)S(1)} %get-tuple-element.18, f32[10,128]{1,0:T(8,128)S(1)} %fusion.65, f32[10,128,4096]{2,1,0:T(8,128)} %fusion.17, pred[128,4096]{1,0:T(8,128)(4,1)} %copy-done.5), kind=kOutput, calls=%fused_computation.11 | convolution fusion | flops 6744724480 | bytes 26933248 | tf_op jit(solution)/shard_map/dot_general | solution.py:85
  164.0 0.0 copy-start.1
  164.0 0.5 multiply_reduce_fusion.3
  164.5 0.4 copy-done.1
  165.0 0.3 multiply_reduce_fusion.2
  165.3 0.3 multiply_convert_fusion.2
  165.6 18.9 %all-gather.8.cloned.1.call-done = bf16[10304,125]{1,0:T(8,128)(2,1)} async-done(((bf16[1288,125]{1,0:T(8,128)(2,1)}), bf16[10304,125]{1,0:T(8,128)(2,1)}) %all-gather.8.cloned.1.call-update) | async-done | bytes 2576016 | tf_op jit(solution)/shard_map/all_gather | solution.py:60
  184.5 0.2 stack.2
  184.7 0.0 copy-start.11
  184.7 36.4 %all_to_all.5 = bf16[8,128,1280]{2,1,0:T(8,128)(2,1)S(1)} all-to-all(bf16[8,128,1280]{2,1,0:T(8,128)(2,1)S(1)} %stack.2), channel_id=1, replica_groups=mesh['dp'=8,'tensor'=32] {'dp'}, dimensions={0} | all-to-all | bytes 5242880 | tf_op jit(solution)/shard_map/all_to_all | solution.py:98
  221.1 1.5 copy-done.3
  222.6 3.7 fusion.66
  226.4 8.9 %convolution_convert_fusion = bf16[1024,1280]{1,0:T(8,128)(2,1)} fusion(bf16[640,1280]{1,0:T(8,128)(2,1)S(1)} %copy-done, f32[1024,640]{1,0:T(8,128)} %fusion.66, bf16[1024,1280]{1,0:T(8,128)(2,1)} %bitcast.64, bf16[1280,640]{1,0:T(8,128)(2,1)} %param.23, f32[640]{0:T(1024)S(1)} %copy-done.12, f32[640]{0:T(1024)S(1)} %copy-done.13), kind=kOutput, calls=%fused_computation.10 | convolution fusion | flops 3361996800 | bytes 11146240 | tf_op jit(solution)/shard_map/dot_general | solution.py:104
  235.3 0.0 reduce-scatter.2.cloned.1.call-update
  235.3 0.1 convert_reduce_fusion.1
  235.5 0.2 reduce-window.8
  235.7 0.1 select_reduce_fusion.1
  235.8 0.7 slice_convert_fusion.2
  236.5 126.3 %reduce-scatter.2.cloned.1.call-done = bf16[128,1280]{1,0:T(8,128)(2,1)} async-done(((bf16[1024,1280]{1,0:T(8,128)(2,1)}), bf16[128,1280]{1,0:T(8,128)(2,1)}) %reduce-scatter.2.cloned.1.call-update) | async-done | bytes 327696 | tf_op jit(solution)/shard_map/reduce_scatter | solution.py:103
  362.8 1.1 fusion.29
  363.9 1.3 multiply_reduce_fusion.1
  365.2 1.4 multiply_convert_fusion.1
  366.6 0.0 copy-start.2
  366.6 0.0 copy-start.14
  366.6 0.2 fusion.12
  366.8 0.2 fusion.13
  367.0 45.6 %all_gather.24 = bf16[32,8,1280]{2,1,0:T(8,128)(2,1)S(1)} all-gather(bf16[1,8,1280]{2,1,0:T(8,128)(2,1)S(1)} %pad_maximum_fusion.1), channel_id=1, replica_groups=mesh['dp'=8,'tensor'=32] {'tensor'}, dimensions={0}, use_global_device_ids=true | all-gather | bytes 675840 | tf_op jit(solution)/shard_map/all_gather | solution.py:129
  412.6 0.1 convert_reduce_fusion
  412.7 0.2 fusion.39
  412.9 0.1 tile.21
  413.0 2.3 fusion.22
  415.3 0.1 tile.9
  415.4 0.1 pad_maximum_fusion.2
  415.5 73.0 %pmax.7 = f32[64]{0:T(128)S(1)} all-reduce(f32[64]{0:T(128)S(1)} %pad_maximum_fusion.2), channel_id=1, replica_groups=mesh['dp'=8,'tensor'=32] {'dp','tensor'}, use_global_device_ids=true, to_apply=%region_17.18 | all-reduce | flops 64 | bytes 512 | tf_op jit(solution)/shard_map/pmax | solution.py:151
  488.5 0.7 convolution_bitcast_fusion.1
  489.2 0.7 convolution_bitcast_fusion
  (41 shorter events, 0.3 us)
Async XLA Ops:
  7.2 219.2 %copy-start = (bf16[640,1280]{1,0:T(8,128)(2,1)S(1)}, bf16[640,1280]{1,0:T(8,128)(2,1)}, u32[]{:S(2)}) copy-start(bf16[640,1280]{1,0:T(8,128)(2,1)} %param.26) | copy-start | bytes 4915204
  7.2 86.3 %all-gather.6.cloned.1.call-start = ((), (), s32[]{:S(2)}) async-start(), calls=%async_computation.3 | async-start | bytes 10813440 | tf_op jit(solution)/shard_map/all_gather | solution.py:55
  11.9 3.3 copy-start.9
  13.9 3.2 copy-start.10
  14.8 5.4 %copy-start.8 = (s32[1,128]{1,0:T(1,128)S(1)}, s32[1,128]{1,0:T(1,128)}, u32[]{:S(2)}) copy-start(s32[1,128]{1,0:T(1,128)} %param.16) | copy-start | bytes 1540
  17.1 167.4 %all-gather.8.cloned.1.call-start = ((), (), s32[]{:S(2)}) async-start(), calls=%async_computation.4 | async-start | bytes 2967552 | tf_op jit(solution)/shard_map/all_gather | solution.py:60
  66.9 50.4 %copy-start.5 = (pred[128,4096]{1,0:T(8,128)(4,1)}, pred[128,4096]{1,0:T(8,128)(4,1)S(1)}, u32[]{:S(2)}) copy-start(pred[128,4096]{1,0:T(8,128)(4,1)S(1)} %fusion.14) | copy-start | bytes 1572868
  103.1 259.7 %reduce-scatter.2.cloned.1.call-start = ((), (), s32[]{:S(2)}) async-start(), calls=%async_computation.2 | async-start | bytes 2949120 | tf_op jit(solution)/shard_map/reduce_scatter | solution.py:103
  138.6 25.4 %copy-start.4 = (bf16[640,1280]{1,0:T(8,128)(2,1)S(1)}, bf16[640,1280]{1,0:T(8,128)(2,1)}, u32[]{:S(2)}) copy-start(bf16[640,1280]{1,0:T(8,128)(2,1)} %param.20) | copy-start | bytes 4915204
  138.6 25.9 %copy-start.6 = (f32[1280]{0:T(1024)S(1)}, f32[1280]{0:T(1024)}, u32[]{:S(2)}) copy-start(f32[1280]{0:T(1024)} %param.21) | copy-start | bytes 15364
  164.0 1.0 copy-start.1
  184.7 37.9 %copy-start.11 = (bf16[1280,640]{1,0:T(8,128)(2,1)S(1)}, bf16[1280,640]{1,0:T(8,128)(2,1)}, u32[]{:S(2)}) copy-start(bf16[1280,640]{1,0:T(8,128)(2,1)} %param.22) | copy-start | bytes 4915204
  221.1 1.5 copy-start.3
  222.6 3.8 copy-start.12
  222.6 3.8 copy-start.13
  235.3 128.6 %copy-start.7 = (f32[1280]{0:T(1024)S(1)}, f32[1280]{0:T(1024)}, u32[]{:S(2)}) copy-start(f32[1280]{0:T(1024)} %param.27) | copy-start | bytes 15364
  366.6 123.4 %copy-start.2 = (bf16[128,1280]{1,0:T(8,128)(2,1)}, bf16[128,1280]{1,0:T(8,128)(2,1)S(1)}, u32[]{:S(2)}) copy-start(bf16[128,1280]{1,0:T(8,128)(2,1)S(1)} %multiply_convert_fusion.1) | copy-start | bytes 983044
  366.6 121.9 %copy-start.14 = (s32[32]{0:T(128)S(1)}, s32[32]{0:T(128)}, u32[]{:S(2)}) copy-start(s32[32]{0:T(128)} %param.17) | copy-start | bytes 388
Sparse Core Ops, SparseCore 0:
  17.2 76.2 all-gather.5
  103.2 81.2 all-gather.7
  235.4 127.2 reduce-scatter.1
